TPU v7x, 256 devices: a whole 4x4x8 slice. The times are simulated.
256 devices in a mesh: ctx: 8 (over x, z_lo), tp: 32 (over z_hi, y, core).
Axes of the slice: x: 4, y: 4, z: 8 (z_hi: 4, z_lo: 2; z = z_hi * 2 + z_lo), core: 2. Of those that a mesh axis runs over, the one named last changes fastest.
Arguments:
- states: bfloat16 [8192, 2048], P(('ctx', 'tp')), may hold values from -6 to 6
- short_lengths: int32 [64], P('ctx'), may hold values from 1 to 64, 3072 in all
- attn_gain: float32 [2048], replicated, may hold values from 0.5 to 16
- wq: bfloat16 [2048, 2048], P(None, 'tp'), may hold values from -0.125 to 0.125
- wkv: bfloat16 [2048, 512], replicated, may hold values from -0.125 to 0.125
- wo: bfloat16 [2048, 2048], P('tp'), may hold values from -0.125 to 0.125
- mlp_gain: float32 [2048], replicated, may hold values from 0.5 to 1.5
- w_gate: bfloat16 [2048, 5632], P(None, 'tp'), may hold values from -0.125 to 0.125
- w_up: bfloat16 [2048, 5632], P(None, 'tp'), may hold values from -0.125 to 0.125
- w_down: bfloat16 [5632, 2048], P('tp'), may hold values from -0.078125 to 0.078125
Outputs:
- updated: bfloat16 [8192, 2048], P(('ctx', 'tp'))
- long_cache: bfloat16 [2, 2048, 512], P(None, 'ctx', 'tp')
- short_cache: bfloat16 [64, 64, 512], P('ctx', None, 'tp')
Inputs may be any that keep to these rules, and one draw needn't show every extreme that they name: `short_lengths`: rows of a short prompt at or beyond its length are padding; the largest length is 64.
All inputs are finite; a program needn't handle non-finite values. No bound on the sum of `short_lengths` on one device may be relied on, other than what follows from the above.
Results may differ from a plain program's by a relative error of at most 0.022.
The roundings to bfloat16 on the way count: a program that leaves them out, or rounds other values in their place, can miss the bound.
Values may be sent and summed in bfloat16 or wider, within the bound.
No kernel may reach another device: no remote copies, remote signals or barrier semaphores. Data moves between devices by JAX's collectives and lax.ppermute only.
A program may use at most 64 MiB of HBM per device.

v0:
```python
import jax
import jax.numpy as jnp
from jax import lax
from jax.sharding import PartitionSpec as P

KVH = 4
HEAD_SIZE = 64
LONG = 2
LLEN = 2048
SLEN = 64
EPS = 1e-05
THETA = 10000.0
NEG = -1e30


def rms_scale(matrix, gain):
    entries = matrix.astype(jnp.float32)
    power = jnp.mean(entries * entries, axis=-1, keepdims=True)
    return (entries * lax.rsqrt(power + EPS) * gain).astype(jnp.bfloat16)


def rotate(entries, positions):
    half_width = entries.shape[-1] // 2
    frequency = THETA ** (-jnp.arange(half_width, dtype=jnp.float32) * 2.0 / entries.shape[-1])
    angles = positions.astype(jnp.float32)[:, None] * frequency[None, :]
    cosine = jnp.cos(angles)[:, None, :]
    sine_wave = jnp.sin(angles)[:, None, :]
    first_half = entries[..., :half_width]
    second_half = entries[..., half_width:]
    return jnp.concatenate(
        [
            first_half * cosine - second_half * sine_wave,
            second_half * cosine + first_half * sine_wave,
        ],
        axis=-1,
    )


def rank_positions(ctx_rank, rank_rows, block_len, long_rows, n_blocks):
    index_row = jnp.arange(rank_rows, dtype=jnp.int32)
    half_index = index_row // block_len % 2
    offset_row = index_row % block_len
    which_block = jnp.where(half_index == 0, ctx_rank, n_blocks - 1 - ctx_rank)
    long_pos = which_block * block_len + offset_row
    short_pos = (index_row - long_rows) % SLEN
    return jnp.where(index_row < long_rows, long_pos, short_pos)


def project(matrix, positions, wq, wkv_head, heads_dev):
    row_count = matrix.shape[0]
    query_matrix = jnp.dot(matrix, wq, preferred_element_type=jnp.float32).reshape(
        row_count, heads_dev, HEAD_SIZE
    )
    query_matrix = rotate(query_matrix, positions).astype(jnp.bfloat16)
    pairs = jnp.dot(matrix, wkv_head, preferred_element_type=jnp.float32)
    key_matrix = rotate(pairs[:, None, :HEAD_SIZE], positions).astype(jnp.bfloat16)[:, 0]
    value_matrix = pairs[:, HEAD_SIZE:].astype(jnp.bfloat16)
    return jnp.concatenate(
        [query_matrix.reshape(row_count, heads_dev * HEAD_SIZE), key_matrix, value_matrix], axis=1
    )


def attend(soft_state, query_matrix, query_pos, key_matrix, value_matrix, key_pos, valid_keys):
    best_score, weight_sum, weighted = soft_state
    logit_scores = jnp.einsum(
        "rzsm,rvm->rzsv", query_matrix, key_matrix, preferred_element_type=jnp.float32
    ) * HEAD_SIZE ** (-0.5)
    allowed = (key_pos[None, :] <= query_pos[:, None])[None, None] & valid_keys[:, None, None, :]
    logit_scores = jnp.where(allowed, logit_scores, NEG)
    new_best = jnp.maximum(best_score, jnp.max(logit_scores, axis=-1))
    weights = jnp.where(allowed, jnp.exp(logit_scores - new_best[..., None]), 0.0)
    weight_sum = jnp.sum(weights, axis=-1)
    weighted = jnp.einsum(
        "awlp,ape->awle",
        weights.astype(jnp.bfloat16),
        value_matrix,
        preferred_element_type=jnp.float32,
    )
    return (new_best, weight_sum, weighted)


def per_device(states, short_lengths, attn_gain, wq, wkv, wo, mlp_gain, w_gate, w_up, w_down):
    n_ctx = lax.axis_size("ctx")
    n_tp = lax.axis_size("tp")
    ctx_rank = lax.axis_index("ctx")
    tp_index = lax.axis_index("tp")
    tok_rows = states.shape[0]
    rank_rows = tok_rows * n_tp
    n_blocks = 2 * n_ctx
    block_len = LLEN // n_blocks
    long_rows = LONG * 2 * block_len
    heads_dev = wq.shape[1] // HEAD_SIZE
    q_cols = heads_dev * HEAD_SIZE
    pair_width = 2 * HEAD_SIZE
    cache_cols = KVH * pair_width // n_tp
    kv_group = tp_index * KVH // n_tp
    wkv_head = lax.dynamic_slice_in_dim(wkv, kv_group * pair_width, pair_width, 1)
    first_col = tp_index * cache_cols - kv_group * pair_width
    positions = rank_positions(ctx_rank, rank_rows, block_len, long_rows, n_blocks)
    packed = project(
        lax.all_gather(rms_scale(states, attn_gain), "tp", axis=0, tiled=True),
        positions,
        wq,
        wkv_head,
        heads_dev,
    )
    query_matrix = packed[:, :q_cols].reshape(rank_rows, heads_dev, HEAD_SIZE)
    key_matrix = packed[:, q_cols : q_cols + HEAD_SIZE]
    value_matrix = packed[:, q_cols + HEAD_SIZE :]
    long_q = (
        query_matrix[:long_rows]
        .reshape(LONG, 2 * block_len, heads_dev, HEAD_SIZE)
        .transpose(0, 2, 1, 3)
    )
    long_k = key_matrix[:long_rows].reshape(LONG, 2, 1, block_len, HEAD_SIZE)
    long_v = value_matrix[:long_rows].reshape(LONG, 2, 1, block_len, HEAD_SIZE)
    long_qpos = positions[: 2 * block_len]
    half_pick = jnp.arange(2, dtype=jnp.int32)[:, None, None]
    long_init = (
        jnp.full((LONG, heads_dev, 2 * block_len), NEG, jnp.float32),
        jnp.zeros((LONG, heads_dev, 2 * block_len), jnp.float32),
        jnp.zeros((LONG, heads_dev, 2 * block_len, HEAD_SIZE), jnp.float32),
        jnp.zeros((LONG, 2, block_len, cache_cols), jnp.float32),
    )
    piece_k = lax.all_gather(long_k, "ctx", axis=2, tiled=True)
    piece_v = lax.all_gather(long_v, "ctx", axis=2, tiled=True)
    piece_blocks = piece_k.shape[2]
    block_ids = jnp.arange(piece_blocks, dtype=jnp.int32)
    held_blocks = jnp.stack([block_ids, n_blocks - 1 - block_ids])
    key_pos = (
        held_blocks[:, :, None] * block_len + jnp.arange(block_len, dtype=jnp.int32)
    ).reshape(-1)
    key_count = 2 * piece_blocks * block_len
    flat_k = piece_k.reshape(LONG, key_count, HEAD_SIZE)
    flat_v = piece_v.reshape(LONG, key_count, HEAD_SIZE)
    all_valid = jnp.ones((LONG, key_count), dtype=bool)
    soft_state = long_init[:3]
    soft_state = attend(soft_state, long_q, long_qpos, flat_k, flat_v, key_pos, all_valid)
    joined = jnp.concatenate([piece_k, piece_v], axis=-1)
    own_cols = lax.dynamic_slice_in_dim(joined, first_col, cache_cols, 4)
    selector = ((held_blocks[None] // 2 == ctx_rank) & (held_blocks[None] % 2 == half_pick)).astype(
        jnp.bfloat16
    )
    cache_rows = jnp.einsum(
        "ehj,phjbc->pebc", selector, own_cols, preferred_element_type=jnp.float32
    )
    folded = soft_state + (cache_rows,)
    long_out = (
        (folded[2] / folded[1][..., None])
        .astype(jnp.bfloat16)
        .transpose(0, 2, 1, 3)
        .reshape(long_rows, q_cols)
    )
    long_cache = folded[3].astype(jnp.bfloat16).reshape(LONG, 2 * block_len, cache_cols)
    short_count = short_lengths.shape[0]
    short_q = (
        query_matrix[long_rows:]
        .reshape(short_count, SLEN, heads_dev, HEAD_SIZE)
        .transpose(0, 2, 1, 3)
    )
    short_k = key_matrix[long_rows:].reshape(short_count, SLEN, HEAD_SIZE)
    short_v = value_matrix[long_rows:].reshape(short_count, SLEN, HEAD_SIZE)
    offsets = jnp.arange(SLEN, dtype=jnp.int32)
    short_valid = offsets[None, :] < short_lengths[:, None]
    short_init = (
        jnp.full((short_count, heads_dev, SLEN), NEG, jnp.float32),
        jnp.zeros((short_count, heads_dev, SLEN), jnp.float32),
        jnp.zeros((short_count, heads_dev, SLEN, HEAD_SIZE), jnp.float32),
    )
    short_state = attend(short_init, short_q, offsets, short_k, short_v, offsets, short_valid)
    short_out = (
        (short_state[2] / short_state[1][..., None])
        .astype(jnp.bfloat16)
        .transpose(0, 2, 1, 3)
        .reshape(short_count * SLEN, q_cols)
    )
    short_cache = lax.dynamic_slice_in_dim(
        jnp.concatenate([short_k, short_v], axis=-1), first_col, cache_cols, 2
    )
    attn = jnp.concatenate([long_out, short_out], axis=0)
    mixed = lax.psum_scatter(
        jnp.dot(attn, wo, preferred_element_type=jnp.float32).astype(jnp.bfloat16),
        "tp",
        scatter_dimension=0,
        tiled=True,
    ).astype(jnp.float32)
    residual = (states.astype(jnp.float32) + mixed).astype(jnp.bfloat16)
    piece = lax.all_gather(rms_scale(residual, mlp_gain), "tp", axis=0, tiled=True)
    gate = jnp.dot(piece, w_gate, preferred_element_type=jnp.float32)
    up_part = jnp.dot(piece, w_up, preferred_element_type=jnp.float32)
    hidden = (jax.nn.silu(gate) * up_part).astype(jnp.bfloat16)
    down = lax.psum_scatter(
        jnp.dot(hidden, w_down, preferred_element_type=jnp.float32).astype(jnp.bfloat16),
        "tp",
        scatter_dimension=0,
        tiled=True,
    ).astype(jnp.float32)
    updated = (residual.astype(jnp.float32) + down).astype(jnp.bfloat16)
    return (updated, long_cache, short_cache)


def solution(mesh):
    in_specs = (
        P(("ctx", "tp"), None),
        P("ctx"),
        P(),
        P(None, "tp"),
        P(),
        P("tp", None),
        P(),
        P(None, "tp"),
        P(None, "tp"),
        P("tp", None),
    )
    out_specs = (P(("ctx", "tp"), None), P(None, "ctx", "tp"), P("ctx", None, "tp"))
    return jax.shard_map(
        per_device, mesh=mesh, in_specs=in_specs, out_specs=out_specs, check_vma=False
    )
```

profile of v0, /device:TPU:2, one launch (start us, length us, event | category | flops | bytes accessed | tf_op | source)
XLA Modules:
  0.0 431.4 jit_solution(14815538953844404363)
XLA Ops:
  7.2 1.2 fusion.28
  8.4 1.7 fusion.30
  10.2 0.6 and_select_fusion.1
  10.9 1.3 iota_compare_fusion.1
  12.2 1.2 broadcast_compare_fusion
  13.4 61.1 %all-gather.3.cloned.1.call-done = bf16[1024,2048]{1,0:T(8,128)(2,1)} async-done(((bf16[32,2048]{1,0:T(8,128)(2,1)}), bf16[1024,2048]{1,0:T(8,128)(2,1)}) %all-gather.3.cloned.1.call-update) | async-done | bytes 4194320 | tf_op jit(solution)/shard_map/all_gather | solution.py:101
  74.5 3.7 fusion.105
  78.4 3.6 convolution_bitcast_fusion
  82.0 0.6 fusion.52
  83.4 0.5 fusion.8
  84.0 27.9 %all_gather.13 = bf16[2,2,8,128,64]{3,4,1,0,2:T(8,128)(2,1)S(1)} all-gather(bf16[2,2,1,128,64]{3,4,1,0,2:T(8,128)(2,1)S(1)} %copy.33), channel_id=1, replica_groups=mesh['ctx'=8,'tp'=32] {'ctx'}, dimensions={2}, use_global_device_ids=true | all-gather | bytes 589824 | tf_op jit(solution)/shard_map/all_gather | solution.py:125
  111.9 0.3 copy.34
  112.2 30.0 %all_gather.14 = bf16[2,2,8,128,64]{3,4,1,0,2:T(8,128)(2,1)S(1)} all-gather(bf16[2,2,1,128,64]{3,4,1,0,2:T(8,128)(2,1)S(1)} %copy.36), channel_id=1, replica_groups=mesh['ctx'=8,'tp'=32] {'ctx'}, dimensions={2}, use_global_device_ids=true | all-gather | bytes 589824 | tf_op jit(solution)/shard_map/all_gather | solution.py:126
  142.6 1.0 reshape.515
  143.6 1.0 reshape.513
  144.6 2.4 fusion
  147.0 1.4 fusion.1
  148.4 1.1 fusion.17
  149.6 3.2 convolution_convert_fusion.1
  152.9 99.4 %reduce-scatter.3.cloned.1.call-done = bf16[32,2048]{1,0:T(8,128)(2,1)} async-done(((bf16[1024,2048]{1,0:T(8,128)(2,1)}), bf16[32,2048]{1,0:T(8,128)(2,1)}) %reduce-scatter.3.cloned.1.call-update) | async-done | bytes 131088 | tf_op jit(solution)/shard_map/reduce_scatter | solution.py:181
  252.3 1.1 fusion.32
  253.3 1.7 fusion.34
  255.3 58.1 %all-gather.5.cloned.1.call-done = bf16[1024,2048]{1,0:T(8,128)(2,1)} async-done(((bf16[32,2048]{1,0:T(8,128)(2,1)}), bf16[1024,2048]{1,0:T(8,128)(2,1)}) %all-gather.5.cloned.1.call-update) | async-done | bytes 4194320 | tf_op jit(solution)/shard_map/all_gather | solution.py:188
  313.3 4.8 %fusion.106 = f32[1024,176]{0,1:T(8,128)} fusion(bf16[1024,2048]{1,0:T(8,128)(2,1)} %all-gather.5.cloned.1.call-done, bf16[2048,176]{0,1:T(8,128)(2,1)} %param.17), kind=kOutput, calls=%fused_computation.156 | convolution fusion | flops 738197504 | bytes 5636096 | tf_op jit(solution)/shard_map/dot_general | solution.py:189
  318.2 7.5 %convolution_convert_fusion = bf16[1024,2048]{1,0:T(8,128)(2,1)} fusion(bf16[176,2048]{1,0:T(8,128)(2,1)} %param.19, bf16[1024,2048]{1,0:T(8,128)(2,1)} %all-gather.5.cloned.1.call-done, bf16[2048,176]{0,1:T(8,128)(2,1)} %param.18, f32[1024,176]{0,1:T(8,128)} %fusion.106), kind=kOutput, calls=%fused_computation.2 | convolution fusion | flops 1479573504 | bytes 10551296 | tf_op jit(solution)/shard_map/dot_general | solution.py:193
  325.7 0.7 copy.47
  326.4 0.9 copy.46
  327.3 0.9 fusion.10
  328.2 0.6 reshape.519
  328.8 0.6 fusion.68
  329.5 93.7 %reduce-scatter.5.cloned.1.call-done = bf16[32,2048]{1,0:T(8,128)(2,1)} async-done(((bf16[1024,2048]{1,0:T(8,128)(2,1)}), bf16[32,2048]{1,0:T(8,128)(2,1)}) %reduce-scatter.5.cloned.1.call-update) | async-done | bytes 131088 | tf_op jit(solution)/shard_map/reduce_scatter | solution.py:192
  423.2 1.6 fusion.35
  (57 shorter events, 2.0 us)
Async XLA Ops:
  7.2 67.3 %copy-start = (bf16[2048,512]{1,0:T(8,128)(2,1)S(1)}, bf16[2048,512]{1,0:T(8,128)(2,1)}, u32[]{:S(2)}) copy-start(bf16[2048,512]{1,0:T(8,128)(2,1)} %param.14) | copy-start | bytes 6291460
  7.2 67.3 %all-gather.3.cloned.1.call-start = ((), (), s32[]{:S(2)}) async-start(), calls=%async_computation.2 | async-start | bytes 4325376 | tf_op jit(solution)/shard_map/all_gather | solution.py:101
  10.1 242.2 %reduce-scatter.3.cloned.1.call-start = ((), (), s32[]{:S(2)}) async-start(), calls=%async_computation.3 | async-start | bytes 4325376 | tf_op jit(solution)/shard_map/reduce_scatter | solution.py:181
  13.4 65.0 %copy-start.6 = (bf16[2048,64]{0,1:T(8,128)(2,1)S(1)}, bf16[2048,64]{0,1:T(8,128)(2,1)}, u32[]{:S(2)}) copy-start(bf16[2048,64]{0,1:T(8,128)(2,1)} %param.13) | copy-start | bytes 786436
  78.4 4.6 %copy-start.9 = (pred[8,64]{1,0:T(8,128)(4,1)S(1)}, pred[8,64]{1,0:T(8,128)(4,1)}, u32[]{:S(2)}) copy-start(pred[8,64]{1,0:T(8,128)(4,1)} %iota_compare_fusion.1) | copy-start | bytes 1540
  82.8 1.1 copy-start.5
  144.6 2.4 copy-start.1
  144.6 3.8 copy-start.4
  148.4 1.2 copy-start.7
  149.6 102.7 %copy-start.2 = (bf16[32,2048]{1,0:T(8,128)(2,1)S(1)}, bf16[32,2048]{1,0:T(8,128)(2,1)}, u32[]{:S(2)}) copy-start(bf16[32,2048]{1,0:T(8,128)(2,1)} %param.10) | copy-start | bytes 393220
  149.6 103.8 %copy-start.8 = (f32[2048]{0:T(1024)S(1)}, f32[2048]{0:T(1024)}, u32[]{:S(2)}) copy-start(f32[2048]{0:T(1024)} %param.16) | copy-start | bytes 24580
  152.8 160.5 %all-gather.5.cloned.1.call-start = ((), (), s32[]{:S(2)}) async-start(), calls=%async_computation.4 | async-start | bytes 4325376 | tf_op jit(solution)/shard_map/all_gather | solution.py:188
  255.0 168.2 %reduce-scatter.5.cloned.1.call-start = ((), (), s32[]{:S(2)}) async-start(), calls=%async_computation.5 | async-start | bytes 4325376 | tf_op jit(solution)/shard_map/reduce_scatter | solution.py:192
  325.6 97.6 %copy-start.3 = (bf16[32,2048]{1,0:T(8,128)(2,1)S(1)}, bf16[32,2048]{1,0:T(8,128)(2,1)}, u32[]{:S(2)}) copy-start(bf16[32,2048]{1,0:T(8,128)(2,1)} %reduce-scatter.3.cloned.1.call-done) | copy-start | bytes 393220
Sparse Core Ops, SparseCore 0:
  11.1 63.2 all-gather.2
  153.0 99.2 reduce-scatter.2
  255.7 57.5 all-gather.4
  325.8 97.4 reduce-scatter.4
where the time goes:
time: 432 us; the launch traced here: 431 us
  waiting for transfers between devices  312 us (72%)
  blocking collectives  57.9 us (13%)
  matrix products  28 us (6%)
  between operations  14.1 us (3%)
  other arithmetic  13.2 us (3%)
  local copies, waits for them, and re-layouts  5.59 us (1%)
    reduce_scatter x1, waiting for transfers between devices, per_device(): lax.psum_scatter(jnp.dot(attn, wo, preferred_element_type=jnp.float32).as...  99.4 us
    reduce_scatter x1, waiting for transfers between devices, per_device(): lax.psum_scatter(jnp.dot(hidden, w_down, preferred_element_type=jnp.float...  93.7 us
    all_gather x1, waiting for transfers between devices, per_device(): lax.all_gather(rms_scale(states, attn_gain), 'tp', axis=0, tiled=True)  61.1 us
    all_gather x1, waiting for transfers between devices, per_device(): lax.all_gather(rms_scale(residual, mlp_gain), 'tp', axis=0, tiled=True)  58.1 us
    all_gather x1, blocking collectives, per_device(): piece_v = lax.all_gather(long_v, 'ctx', axis=2, tiled=True)  30 us
    all_gather x1, blocking collectives, per_device(): piece_k = lax.all_gather(long_k, 'ctx', axis=2, tiled=True)  27.9 us
  transfers between devices with their start and end apart: 4, of which 4 were waited for; matrix products, arithmetic and copies ran while one was open for 2% of the time, Pallas kernels for 0%

commit v1 on v0

--- a/solution.py
+++ b/solution.py
@@ -98,7 +98,12 @@
     first_col = tp_index * cache_cols - kv_group * pair_width
     positions = rank_positions(ctx_rank, rank_rows, block_len, long_rows, n_blocks)
     packed = project(
-        lax.all_gather(rms_scale(states, attn_gain), "tp", axis=0, tiled=True),
+        jnp.concatenate(
+            lax.all_to_all(
+                jnp.stack([rms_scale(states, attn_gain)] * lax.axis_size("tp")), "tp", 0, 0
+            ),
+            axis=0,
+        ),
         positions,
         wq,
         wkv_head,

time: 432 us -> 478 us (1.11)
  waiting for transfers between devices: 312 us -> 344 us
  starting transfers between devices: 0.34 us -> 12.1 us
    all_to_all x0 -> x1, waiting for transfers between devices: none -> 93.6 us  [per_device(): lax.all_to_all(jnp.stack([rms_scale(states, attn_gain)] * lax.axis_size('...]
    all_gather x1 -> x0, waiting for transfers between devices: 61.1 us -> none  [per_device(): lax.all_gather(rms_scale(states, attn_gain), 'tp', axis=0, tiled=True)]
    all_to_all x0 -> x1, starting transfers between devices: none -> 11.7 us  [per_device(): lax.all_to_all(jnp.stack([rms_scale(states, attn_gain)] * lax.axis_size('...]
  transfers between devices with their start and end apart: 4 -> 4, of which waited for: 4 -> 4; matrix products, arithmetic and copies ran while one was open for 2% -> 1% of each run, Pallas kernels for 0% -> 0%
where the time goes in v1:
time: 478 us
  waiting for transfers between devices  344 us (72%)
  blocking collectives  57.7 us (12%)
  matrix products  29.3 us (6%)
  between operations  14.1 us (3%)
  other arithmetic  12.6 us (3%)
  starting transfers between devices  12.1 us (3%)
  local copies, waits for them, and re-layouts  8.09 us (2%)
    reduce_scatter x1, waiting for transfers between devices, per_device(): lax.psum_scatter(jnp.dot(attn, wo, preferred_element_type=jnp.float32).as...  98.7 us
    reduce_scatter x1, waiting for transfers between devices, per_device(): lax.psum_scatter(jnp.dot(hidden, w_down, preferred_element_type=jnp.float...  93.7 us
    all_to_all x1, waiting for transfers between devices, per_device(): lax.all_to_all(jnp.stack([rms_scale(states, attn_gain)] * lax.axis_size('...  93.6 us
    all_gather x1, waiting for transfers between devices, per_device(): lax.all_gather(rms_scale(residual, mlp_gain), 'tp', axis=0, tiled=True)  58 us
    all_gather x1, blocking collectives, per_device(): piece_v = lax.all_gather(long_v, 'ctx', axis=2, tiled=True)  30 us
    all_gather x1, blocking collectives, per_device(): piece_k = lax.all_gather(long_k, 'ctx', axis=2, tiled=True)  27.7 us
    all_to_all x1, starting transfers between devices, per_device(): lax.all_to_all(jnp.stack([rms_scale(states, attn_gain)] * lax.axis_size('...  11.7 us
  transfers between devices with their start and end apart: 4, of which 4 were waited for; matrix products, arithmetic and copies ran while one was open for 1% of the time, Pallas kernels for 0%

profile of v1, /device:TPU:2, one launch (start us, length us, event | category | flops | bytes accessed | tf_op | source)
XLA Modules:
  0.0 477.8 jit_solution(8010109845379656204)
XLA Ops:
  7.2 1.2 fusion.28
  8.4 1.0 fusion.30
  9.4 2.5 stack.5
  11.9 11.7 %all-to-all-start = ((bf16[32,32,2048]{2,1,0:T(8,128)(2,1)}), bf16[32,32,2048]{2,1,0:T(8,128)(2,1)}, u32[]{:S(2)}, u32[]{:S(2)}) async-start(bf16[32,32,2048]{2,1,0:T(8,128)(2,1)} %stack.5), calls=%async_computation | async-start | bytes 8388608 | tf_op jit(solution)/shard_map/all_to_all | solution.py:102
  24.4 0.6 iota_compare_fusion.1
  25.1 1.2 broadcast_compare_fusion
  26.3 93.6 %all-to-all-done = bf16[32,32,2048]{2,1,0:T(8,128)(2,1)} async-done(((bf16[32,32,2048]{2,1,0:T(8,128)(2,1)}), bf16[32,32,2048]{2,1,0:T(8,128)(2,1)}, u32[]{:S(2)}, u32[]{:S(2)}) %all-to-all-start) | async-done | bytes 4194336 | tf_op jit(solution)/shard_map/all_to_all | solution.py:102
  119.9 3.6 convolution_bitcast_fusion
  123.5 3.7 fusion.105
  128.4 0.9 fusion.104
  129.3 0.8 fusion.36
  130.2 1.1 fusion.8
  131.4 27.7 %all_gather.9 = bf16[2,2,8,128,64]{3,4,1,0,2:T(8,128)(2,1)S(1)} all-gather(bf16[2,2,1,128,64]{3,4,1,0,2:T(8,128)(2,1)S(1)} %copy.33), channel_id=1, replica_groups=mesh['ctx'=8,'tp'=32] {'ctx'}, dimensions={2}, use_global_device_ids=true | all-gather | bytes 589824 | tf_op jit(solution)/shard_map/all_gather | solution.py:130
  159.5 30.0 %all_gather.10 = bf16[2,2,8,128,64]{3,4,1,0,2:T(8,128)(2,1)S(1)} all-gather(bf16[2,2,1,128,64]{3,4,1,0,2:T(8,128)(2,1)S(1)} %copy.36), channel_id=1, replica_groups=mesh['ctx'=8,'tp'=32] {'ctx'}, dimensions={2}, use_global_device_ids=true | all-gather | bytes 589824 | tf_op jit(solution)/shard_map/all_gather | solution.py:131
  189.8 1.0 reshape.521
  190.9 1.0 reshape.519
  191.9 2.4 fusion
  194.3 1.4 fusion.1
  195.7 1.1 fusion.17
  196.9 3.2 convolution_convert_fusion.1
  200.2 98.7 %reduce-scatter.3.cloned.1.call-done = bf16[32,2048]{1,0:T(8,128)(2,1)} async-done(((bf16[1024,2048]{1,0:T(8,128)(2,1)}), bf16[32,2048]{1,0:T(8,128)(2,1)}) %reduce-scatter.3.cloned.1.call-update) | async-done | bytes 131088 | tf_op jit(solution)/shard_map/reduce_scatter | solution.py:186
  298.9 1.1 fusion.32
  299.9 1.7 fusion.34
  301.8 58.0 %all-gather.2.cloned.1.call-done = bf16[1024,2048]{1,0:T(8,128)(2,1)} async-done(((bf16[32,2048]{1,0:T(8,128)(2,1)}), bf16[1024,2048]{1,0:T(8,128)(2,1)}) %all-gather.2.cloned.1.call-update) | async-done | bytes 4194320 | tf_op jit(solution)/shard_map/all_gather | solution.py:193
  359.8 4.8 %fusion.106 = f32[1024,176]{0,1:T(8,128)} fusion(bf16[1024,2048]{1,0:T(8,128)(2,1)} %all-gather.2.cloned.1.call-done, bf16[2048,176]{0,1:T(8,128)(2,1)} %param.17), kind=kOutput, calls=%fused_computation.156 | convolution fusion | flops 738197504 | bytes 5636096 | tf_op jit(solution)/shard_map/dot_general | solution.py:194
  364.6 7.5 %convolution_convert_fusion = bf16[1024,2048]{1,0:T(8,128)(2,1)} fusion(bf16[176,2048]{1,0:T(8,128)(2,1)} %param.19, bf16[1024,2048]{1,0:T(8,128)(2,1)} %all-gather.2.cloned.1.call-done, bf16[2048,176]{0,1:T(8,128)(2,1)} %param.18, f32[1024,176]{0,1:T(8,128)} %fusion.106), kind=kOutput, calls=%fused_computation.2 | convolution fusion | flops 1479573504 | bytes 10551296 | tf_op jit(solution)/shard_map/dot_general | solution.py:198
  372.1 0.7 copy.47
  372.8 0.9 copy.46
  373.8 0.9 fusion.10
  375.3 0.6 fusion.68
  376.0 93.7 %reduce-scatter.5.cloned.1.call-done = bf16[32,2048]{1,0:T(8,128)(2,1)} async-done(((bf16[1024,2048]{1,0:T(8,128)(2,1)}), bf16[32,2048]{1,0:T(8,128)(2,1)}) %reduce-scatter.5.cloned.1.call-update) | async-done | bytes 131088 | tf_op jit(solution)/shard_map/reduce_scatter | solution.py:197
  469.6 1.6 fusion.35
  (57 shorter events, 3.7 us)
Async XLA Ops:
  7.2 116.3 %copy-start = (bf16[2048,512]{1,0:T(8,128)(2,1)S(1)}, bf16[2048,512]{1,0:T(8,128)(2,1)}, u32[]{:S(2)}) copy-start(bf16[2048,512]{1,0:T(8,128)(2,1)} %param.14) | copy-start | bytes 6291460
  11.9 12.5 %copy-start.9 = (s32[8]{0:T(128)S(1)}, s32[8]{0:T(128)}, u32[]{:S(2)}) copy-start(s32[8]{0:T(128)} %param.11) | copy-start | bytes 100
  11.9 108.0 %copy-start.6 = (bf16[2048,64]{0,1:T(8,128)(2,1)S(1)}, bf16[2048,64]{0,1:T(8,128)(2,1)}, u32[]{:S(2)}) copy-start(bf16[2048,64]{0,1:T(8,128)(2,1)} %param.13) | copy-start | bytes 786436
  11.9 108.0 %all-to-all-start = ((bf16[32,32,2048]{2,1,0:T(8,128)(2,1)}), bf16[32,32,2048]{2,1,0:T(8,128)(2,1)}, u32[]{:S(2)}, u32[]{:S(2)}) async-start(bf16[32,32,2048]{2,1,0:T(8,128)(2,1)} %stack.5), calls=%async_computation | async-start | bytes 8388608 | tf_op jit(solution)/shard_map/all_to_all | solution.py:102
  23.6 275.2 %reduce-scatter.3.cloned.1.call-start = ((), (), s32[]{:S(2)}) async-start(), calls=%async_computation.3 | async-start | bytes 4325376 | tf_op jit(solution)/shard_map/reduce_scatter | solution.py:186
  128.2 3.2 copy-start.5
  191.9 2.4 copy-start.1
  191.9 3.8 copy-start.4
  195.7 1.2 copy-start.7
  196.9 102.0 %copy-start.2 = (bf16[32,2048]{1,0:T(8,128)(2,1)S(1)}, bf16[32,2048]{1,0:T(8,128)(2,1)}, u32[]{:S(2)}) copy-start(bf16[32,2048]{1,0:T(8,128)(2,1)} %param.10) | copy-start | bytes 393220
  196.9 103.1 %copy-start.8 = (f32[2048]{0:T(1024)S(1)}, f32[2048]{0:T(1024)}, u32[]{:S(2)}) copy-start(f32[2048]{0:T(1024)} %param.16) | copy-start | bytes 24580
  200.1 159.7 %all-gather.2.cloned.1.call-start = ((), (), s32[]{:S(2)}) async-start(), calls=%async_computation.4 | async-start | bytes 4325376 | tf_op jit(solution)/shard_map/all_gather | solution.py:193
  301.6 168.0 %reduce-scatter.5.cloned.1.call-start = ((), (), s32[]{:S(2)}) async-start(), calls=%async_computation.5 | async-start | bytes 4325376 | tf_op jit(solution)/shard_map/reduce_scatter | solution.py:197
  372.1 97.6 %copy-start.3 = (bf16[32,2048]{1,0:T(8,128)(2,1)S(1)}, bf16[32,2048]{1,0:T(8,128)(2,1)}, u32[]{:S(2)}) copy-start(bf16[32,2048]{1,0:T(8,128)(2,1)} %reduce-scatter.3.cloned.1.call-done) | copy-start | bytes 393220
Sparse Core Ops, SparseCore 0:
  200.2 98.5 reduce-scatter.2
  302.3 57.4 all-gather.1
  372.2 97.3 reduce-scatter.4
